TPU v7x, 256 devices: a whole 4x4x8 slice. The times are simulated.
256 devices in a mesh: wave: 8 (over z_hi, x), region: 32 (over z_lo, y, core).
Axes of the slice: x: 4, y: 4, z: 8 (z_hi: 2, z_lo: 4; z = z_hi * 4 + z_lo), core: 2. Of those that a mesh axis runs over, the one named last changes fastest.
Arguments:
- object_field: float32 [2, 16384, 1024], P(None, 'region'), may hold values from -5 to 5
- probes: float32 [8, 2, 256, 256], P('wave'), may hold values from -5 to 5
- patterns: bfloat16 [8, 512, 256, 256], P('wave', 'region'), may hold values from 0 to 2
- offsets: int32 [512, 2], P('region'), may hold values from 0 to 768, as said below
- counts: int32 [32], P('region'), may hold values from 1 to 16, as said below
Outputs:
- object_grad: float32 [2, 16384, 1024], P(None, 'region', 'wave')
- probe_grad: float32 [8, 2, 256, 256], P('wave')
Inputs may be any that keep to these rules, and one draw needn't show every extreme that they name: Offsets are whole cells: row offsets below 512, column offsets at most 768. `counts`: some tile uses all slots and some tile uses one.
All inputs are finite; a program needn't handle non-finite values.
Results may differ from a plain program's by a relative error of at most 0.0052.
Values sent between devices are 32-bit elements; how exact they have to be, the bound alone decides.
No kernel may reach another device: no remote copies, remote signals or barrier semaphores. Data moves between devices by JAX's collectives and lax.ppermute only.
A program may use at most 128 MiB of HBM per device.

v0:
```python
import math

import jax
import jax.numpy as jnp
from jax import lax
from jax.experimental import pallas as pl
from jax.experimental.pallas import tpu as pltpu
from jax.sharding import PartitionSpec as P

SUB = 8
LANE = 128


def from_behind(block, axis, distance):
    devices = range(lax.axis_size(axis))
    route = [(i - distance, i) for i in devices if i - distance in devices]
    return lax.ppermute(block, axis, route)


def xor_route(axis, bit):
    return [(i, i ^ (1 << bit)) for i in range(lax.axis_size(axis))]


def sum_over(block, axis):
    for bit in range(lax.axis_size(axis).bit_length() - 1):
        block = block + lax.ppermute(block, axis, xor_route(axis, bit))
    return block


def sum_scatter_blocks(held, axis):
    bits = lax.axis_size(axis).bit_length() - 1
    held = held.reshape((2,) * bits + held.shape[1:])
    for bit in range(bits):
        place = bits - 1 - bit
        kept = lax.index_in_dim(held, 0, place, keepdims=False)
        sent = lax.index_in_dim(held, 1, place, keepdims=False)
        held = kept + lax.ppermute(sent, axis, xor_route(axis, bit))
    return held


def windows(offsets, patch_side, width_cols):
    rows = offsets[:, 0]
    cols = offsets[:, 1]
    base = (rows // SUB) * SUB
    down = rows - base
    start = jnp.minimum((cols // LANE) * LANE, width_cols - patch_side - LANE)
    shift = cols - start
    return base, down, start, shift


def extract_kernel(base_ref, down_ref, start_ref, shift_ref, ext_ref, out_ref):
    s = pl.program_id(0)
    side = out_ref.shape[-1]
    high = side + SUB
    wide = side + LANE
    base = pl.multiple_of(base_ref[s], SUB)
    start = pl.multiple_of(start_ref[s], LANE)
    up = (high - down_ref[s]) % high
    left = (wide - shift_ref[s]) % wide
    for c in range(2):
        win = ext_ref[c, pl.ds(base, high), pl.ds(start, wide)]
        win = pltpu.roll(win, up, 0)
        win = pltpu.roll(win, left, 1)
        out_ref[0, c] = win[:side, :side]


def extract_patches(extended, base, down, start, shift, patch_side):
    slots = base.shape[0]
    grid_spec = pltpu.PrefetchScalarGridSpec(
        num_scalar_prefetch=4,
        grid=(slots,),
        in_specs=[pl.BlockSpec(extended.shape, lambda s, *_: (0, 0, 0))],
        out_specs=pl.BlockSpec((1, 2, patch_side, patch_side), lambda s, *_: (s, 0, 0, 0)),
    )
    return pl.pallas_call(
        extract_kernel,
        grid_spec=grid_spec,
        out_shape=jax.ShapeDtypeStruct((slots, 2, patch_side, patch_side), jnp.float32),
        compiler_params=pltpu.CompilerParams(vmem_limit_bytes=48 * 1024 * 1024),
    )(base, down, start, shift, extended)


def accumulate_kernel(base_ref, down_ref, shift_ref, place_ref, count_ref, terms_ref, out_ref, pad_ref):
    s = pl.program_id(0)
    side = terms_ref.shape[-1]
    high = side + SUB
    spans = place_ref.shape[1]

    @pl.when(s == 0)
    def _():
        out_ref[...] = jnp.zeros_like(out_ref)
        pad_ref[...] = jnp.zeros_like(pad_ref)

    @pl.when(s < count_ref[0])
    def _():
        base = pl.multiple_of(base_ref[s], SUB)
        down = down_ref[s]
        shift = shift_ref[s]
        for c in range(2):
            pad_ref[:side, :side] = terms_ref[0, c]
            term = pltpu.roll(pad_ref[...], down, 0)
            term = pltpu.roll(term, shift, 1)
            for k in range(spans):
                out_ref[place_ref[s, k], c, pl.ds(base, high), :] += term[:, k * LANE:(k + 1) * LANE]


def accumulate_terms(terms, base, down, shift, place, count, blocks, rows_out):
    slots, _, side, _ = terms.shape
    grid_spec = pltpu.PrefetchScalarGridSpec(
        num_scalar_prefetch=5,
        grid=(slots,),
        in_specs=[pl.BlockSpec((1, 2, side, side), lambda s, *_: (s, 0, 0, 0))],
        out_specs=pl.BlockSpec((blocks, 2, rows_out, LANE), lambda s, *_: (0, 0, 0, 0)),
        scratch_shapes=[pltpu.VMEM((side + SUB, side + LANE), jnp.float32)],
    )
    return pl.pallas_call(
        accumulate_kernel,
        grid_spec=grid_spec,
        out_shape=jax.ShapeDtypeStruct((blocks, 2, rows_out, LANE), jnp.float32),
        compiler_params=pltpu.CompilerParams(vmem_limit_bytes=48 * 1024 * 1024),
    )(base, down, shift, place, count, terms)


def fused_kernel(base_ref, down_ref, start_ref, shift_ref, place_ref, count_ref,
                 ext_ref, probe_ref, pattern_ref, cos_ref, sin_ref, grad_ref, prb_ref, pad_ref):
    s = pl.program_id(0)
    side = probe_ref.shape[-1]
    high = side + SUB
    wide = side + LANE
    spans = place_ref.shape[1]

    @pl.when(s == 0)
    def _():
        grad_ref[...] = jnp.zeros_like(grad_ref)
        prb_ref[...] = jnp.zeros_like(prb_ref)
        pad_ref[...] = jnp.zeros_like(pad_ref)

    @pl.when(s < count_ref[0])
    def _():
        base = pl.multiple_of(base_ref[s], SUB)
        start = pl.multiple_of(start_ref[s], LANE)
        down = down_ref[s]
        shift = shift_ref[s]
        up = (high - down) % high
        left = (wide - shift) % wide
        cut = []
        for c in range(2):
            win = ext_ref[c, pl.ds(base, high), pl.ds(start, wide)]
            win = pltpu.roll(win, up, 0)
            win = pltpu.roll(win, left, 1)
            cut.append(win[:side, :side])
        x_re, x_im = cut
        p_re = probe_ref[0]
        p_im = probe_ref[1]
        cos_t = cos_ref[...]
        sin_t = sin_ref[...]

        def left_mul(table, part):
            return jnp.dot(table, part, preferred_element_type=jnp.float32)

        def right_mul(part, table):
            return jnp.dot(part, table, preferred_element_type=jnp.float32)

        wave_re = (p_re * x_re - p_im * x_im).astype(jnp.bfloat16)
        wave_im = (p_re * x_im + p_im * x_re).astype(jnp.bfloat16)
        half_re = (left_mul(cos_t, wave_re) + left_mul(sin_t, wave_im)).astype(jnp.bfloat16)
        half_im = (left_mul(cos_t, wave_im) - left_mul(sin_t, wave_re)).astype(jnp.bfloat16)
        far_re = right_mul(half_re, cos_t) + right_mul(half_im, sin_t)
        far_im = right_mul(half_im, cos_t) - right_mul(half_re, sin_t)
        excess = far_re * far_re + far_im * far_im - pattern_ref[0].astype(jnp.float32)
        back_re = (excess * far_re).astype(jnp.bfloat16)
        back_im = (excess * far_im).astype(jnp.bfloat16)
        inner_re = (left_mul(cos_t, back_re) - left_mul(sin_t, back_im)).astype(jnp.bfloat16)
        inner_im = (left_mul(cos_t, back_im) + left_mul(sin_t, back_re)).astype(jnp.bfloat16)
        chi_re = right_mul(inner_re, cos_t) - right_mul(inner_im, sin_t)
        chi_im = right_mul(inner_im, cos_t) + right_mul(inner_re, sin_t)
        prb_ref[0] += x_re * chi_re + x_im * chi_im
        prb_ref[1] += x_re * chi_im - x_im * chi_re
        terms = (p_re * chi_re + p_im * chi_im, p_re * chi_im - p_im * chi_re)
        for c in range(2):
            pad_ref[:side, :side] = terms[c]
            term = pltpu.roll(pad_ref[...], down, 0)
            term = pltpu.roll(term, shift, 1)
            for k in range(spans):
                grad_ref[place_ref[s, k], c, pl.ds(base, high), :] += term[:, k * LANE:(k + 1) * LANE]


def fused_step(extended, probe, patterns, cos_table, sin_table, base, down, start, shift, place,
               count, blocks, rows_out):
    slots, side, _ = patterns.shape
    whole2 = lambda s, *_: (0, 0)
    whole3 = lambda s, *_: (0, 0, 0)
    grid_spec = pltpu.PrefetchScalarGridSpec(
        num_scalar_prefetch=6,
        grid=(slots,),
        in_specs=[
            pl.BlockSpec(extended.shape, whole3),
            pl.BlockSpec(probe.shape, whole3),
            pl.BlockSpec((1, side, side), lambda s, *_: (s, 0, 0)),
            pl.BlockSpec(cos_table.shape, whole2),
            pl.BlockSpec(sin_table.shape, whole2),
        ],
        out_specs=[
            pl.BlockSpec((blocks, 2, rows_out, LANE), lambda s, *_: (0, 0, 0, 0)),
            pl.BlockSpec(probe.shape, whole3),
        ],
        scratch_shapes=[pltpu.VMEM((side + SUB, side + LANE), jnp.float32)],
    )
    return pl.pallas_call(
        fused_kernel,
        grid_spec=grid_spec,
        out_shape=(
            jax.ShapeDtypeStruct((blocks, 2, rows_out, LANE), jnp.float32),
            jax.ShapeDtypeStruct(probe.shape, jnp.float32),
        ),
        compiler_params=pltpu.CompilerParams(vmem_limit_bytes=60 * 1024 * 1024),
    )(base, down, start, shift, place, count, extended, probe, patterns, cos_table, sin_table)


def make_tables(patch_side):
    index = jnp.arange(patch_side, dtype=jnp.int32)
    phase_int = index[:, None] * index[None, :] % patch_side
    phase = phase_int.astype(jnp.float32) * (2.0 * math.pi / patch_side)
    scale = 1.0 / math.sqrt(patch_side)
    return (
        (jnp.cos(phase) * scale).astype(jnp.bfloat16),
        (jnp.sin(phase) * scale).astype(jnp.bfloat16),
    )


def apply_left(table, field_part):
    return jnp.einsum("kn,bnm->bkm", table, field_part, preferred_element_type=jnp.float32)


def apply_right(field_part, table):
    return jnp.einsum("bkn,nm->bkm", field_part, table, preferred_element_type=jnp.float32)


def on_device(object_field, probes, patterns, offsets, counts):
    tile_rows = object_field.shape[1]
    width_cols = object_field.shape[2]
    patch_side = probes.shape[-1]
    slot_total = offsets.shape[0]
    top_rows = object_field[:, :patch_side, :]
    rim_rows = from_behind(top_rows, "region", -1)
    extended = jnp.concatenate([object_field, rim_rows], axis=1)
    base, down, start, shift = windows(offsets, patch_side, width_cols)
    cos_table, sin_table = make_tables(patch_side)
    blocks = lax.axis_size("wave")
    spans = (patch_side + LANE) // LANE
    first = start // LANE
    place = jnp.bitwise_xor(
        first[:, None] + jnp.arange(spans, dtype=jnp.int32)[None, :], lax.axis_index("wave")
    ).astype(jnp.int32)
    grad_ext, probe_part = fused_step(
        extended, probes[0], patterns[0], cos_table, sin_table, base, down, start, shift, place,
        counts, blocks, tile_rows + patch_side,
    )
    probe_total = sum_over(probe_part, "region")
    arrived = from_behind(grad_ext[:, :, tile_rows:, :], "region", 1)
    tile_grad = grad_ext[:, :, :tile_rows, :] + jnp.pad(
        arrived, ((0, 0), (0, 0), (0, tile_rows - patch_side), (0, 0))
    )
    object_out = sum_scatter_blocks(tile_grad, "wave")
    return (object_out, probe_total[None])


def solution(mesh):
    in_specs = (
        P(None, "region", None),
        P("wave", None, None, None),
        P("wave", "region", None, None),
        P("region", None),
        P("region"),
    )
    out_specs = (P(None, "region", "wave"), P("wave", None, None, None))
    return jax.shard_map(
        on_device, mesh=mesh, in_specs=in_specs, out_specs=out_specs, check_vma=False
    )
```

profile of v0, /device:TPU:8, one launch (start us, length us, event | category | flops | bytes accessed | tf_op | source)
XLA Modules:
  0.0 217.7 jit_solution(10784926405951362650)
XLA Ops:
  0.6 0.0 copy-start.1
  0.6 1.7 slice.35
  2.4 1.9 collective-permute-start
  5.0 1.7 multiply_convert_fusion
  6.7 0.0 copy-done.1
  6.7 0.6 bitcast_subtract_fusion
  7.3 0.7 add_xor_fusion.place_ref
  8.0 19.9 %collective-permute-done = f32[2,256,1024]{2,1,0:T(8,128)} collective-permute-done((f32[2,256,1024]{2,1,0:T(8,128)S(1)}, f32[2,256,1024]{2,1,0:T(8,128)}, u32[]{:S(2)}, u32[]{:S(2)}) %collective-permute-start) | collective-permute-done | bytes 2097184 | tf_op jit(solution)/shard_map/ppermute | solution.py:17
  27.8 6.6 %pad_maximum_fusion.ext_ref = f32[2,768,1024]{2,1,0:T(8,128)} fusion(f32[2,256,1024]{2,1,0:T(8,128)} %collective-permute-done, f32[2,512,1024]{2,1,0:T(8,128)} %param.5), kind=kLoop, calls=%fused_computation | loop fusion | flops 1572864 | bytes 12582912 | tf_op jit(solution)/shard_map/concatenate | solution.py:246
  34.4 36.7 %shard_map.68 = (f32[8,2,768,128]{3,2,1,0:T(8,128)}, f32[2,256,256]{2,1,0:T(8,128)}) custom-call(s32[16]{0:T(128)} %get-tuple-element.13.base_ref, s32[16]{0:T(128)} %get-tuple-element.12.down_ref, s32[16]{0:T(128)} %get-tuple-element.7.start_ref, s32[16]{0:T(128)} %get-tuple-element.6.shift_ref, s32[16,3]{1,0:T(8,128)} %add_xor_fusion.place_ref, ...), custom_call_target="tpu_custom_call" | custom-call | tf_op jit(solution)/shard_map/pallas_call | solution.py:209
  71.1 1.7 slice.37
  72.8 5.1 %collective-permute-start.1 = (f32[8,2,256,128]{3,2,1,0:T(8,128)S(1)}, f32[8,2,256,128]{3,2,1,0:T(8,128)S(1)}, u32[]{:S(2)}, u32[]{:S(2)}) collective-permute-start(f32[8,2,256,128]{3,2,1,0:T(8,128)S(1)} %slice.37), channel_id=1, source_target_pairs={{0,1},{1,2},{2,3},{3,4},{4,5},{5,6},{6,7},{7,8},{8,9},{9,10},{10,1... | collective-permute-start | bytes 6291464 | tf_op jit(solution)/shard_map/ppermute | solution.py:17
  77.9 22.3 %collective-permute-done.1 = f32[8,2,256,128]{3,2,1,0:T(8,128)S(1)} collective-permute-done((f32[8,2,256,128]{3,2,1,0:T(8,128)S(1)}, f32[8,2,256,128]{3,2,1,0:T(8,128)S(1)}, u32[]{:S(2)}, u32[]{:S(2)}) %collective-permute-start.1) | collective-permute-done | bytes 2097184 | tf_op jit(solution)/shard_map/ppermute | solution.py:17
  100.2 2.7 %pad_add_fusion = f32[8,2,512,128]{3,2,1,0:T(8,128)S(1)} fusion(f32[8,2,256,128]{3,2,1,0:T(8,128)S(1)} %collective-permute-done.1, f32[8,2,768,128]{3,2,1,0:T(8,128)} %get-tuple-element.4), kind=kLoop, calls=%fused_computation.1 | loop fusion | flops 1048576 | bytes 10485760 | tf_op jit(solution)/shard_map/add | solution.py:261
  102.9 0.3 fusion.12
  103.2 0.0 copy-start
  103.2 0.1 copy.15
  103.3 1.6 collective-permute-start.2
  104.9 0.0 copy-done
  104.9 0.4 collective-permute-start.5
  105.3 1.5 collective-permute-done.5
  106.8 0.1 add.66
  106.9 0.1 collective-permute-start.6
  107.0 14.2 %collective-permute-done.6 = f32[2,256,256]{2,1,0:T(8,128)S(1)} collective-permute-done((f32[2,256,256]{2,1,0:T(8,128)S(1)}, f32[2,256,256]{2,1,0:T(8,128)S(1)}, u32[]{:S(2)}, u32[]{:S(2)}) %collective-permute-start.6) | collective-permute-done | bytes 524320 | tf_op jit(solution)/shard_map/ppermute | solution.py:26
  121.2 0.1 add.67
  121.3 2.6 %collective-permute-start.7 = (f32[2,256,256]{2,1,0:T(8,128)S(1)}, f32[2,256,256]{2,1,0:T(8,128)S(1)}, u32[]{:S(2)}, u32[]{:S(2)}) collective-permute-start(f32[2,256,256]{2,1,0:T(8,128)S(1)} %add.67), channel_id=1, source_target_pairs={{0,4},{1,5},{2,6},{3,7},{4,0},{5,1},{6,2},{7,3},{8,12},{9,13},{10,... | collective-permute-start | bytes 1572872 | tf_op jit(solution)/shard_map/ppermute | solution.py:26
  123.9 27.7 %collective-permute-done.2 = f32[2,2,2,512,128]{4,3,2,0,1:T(8,128)S(1)} collective-permute-done((f32[2,2,2,512,128]{4,3,2,0,1:T(8,128)S(1)}, f32[2,2,2,512,128]{4,3,2,0,1:T(8,128)S(1)}, u32[]{:S(2)}, u32[]{:S(2)}) %collective-permute-start.2) | collective-permute-done | bytes 2097184 | tf_op jit(solution)/shard_map/ppermute | solution.py:37
  151.6 0.3 fusion
  151.9 0.1 slice_bitcast_fusion
  152.0 3.1 %collective-permute-start.3 = (f32[2,2,512,128]{3,2,1,0:T(8,128)S(1)}, f32[2,2,512,128]{3,2,1,0:T(8,128)S(1)}, u32[]{:S(2)}, u32[]{:S(2)}) collective-permute-start(f32[2,2,512,128]{3,2,1,0:T(8,128)S(1)} %slice_bitcast_fusion), channel_id=1, source_target_pairs={{0,64},{32,96},{64,0},{96,32},{128,192},{160,224},{192,128},{224,1... | collective-permute-start | bytes 3145736 | tf_op jit(solution)/shard_map/ppermute | solution.py:37
  155.1 0.0 collective-permute-done.7
  155.1 0.1 add.68
  155.2 0.1 collective-permute-start.8
  155.3 13.4 %collective-permute-done.8 = f32[2,256,256]{2,1,0:T(8,128)S(1)} collective-permute-done((f32[2,256,256]{2,1,0:T(8,128)S(1)}, f32[2,256,256]{2,1,0:T(8,128)S(1)}, u32[]{:S(2)}, u32[]{:S(2)}) %collective-permute-start.8) | collective-permute-done | bytes 524320 | tf_op jit(solution)/shard_map/ppermute | solution.py:26
  168.7 0.1 add.69
  168.7 0.1 collective-permute-start.9
  168.8 9.6 %collective-permute-done.3 = f32[2,2,512,128]{3,2,1,0:T(8,128)S(1)} collective-permute-done((f32[2,2,512,128]{3,2,1,0:T(8,128)S(1)}, f32[2,2,512,128]{3,2,1,0:T(8,128)S(1)}, u32[]{:S(2)}, u32[]{:S(2)}) %collective-permute-start.3) | collective-permute-done | bytes 1048608 | tf_op jit(solution)/shard_map/ppermute | solution.py:37
  178.5 0.1 fusion.1
  178.6 7.3 %collective-permute-start.4 = (f32[2,512,128]{2,1,0:T(8,128)S(1)}, f32[2,512,128]{2,1,0:T(8,128)S(1)}, u32[]{:S(2)}, u32[]{:S(2)}) collective-permute-start(f32[2,512,128]{2,1,0:T(8,128)S(1)} %slice_bitcast_fusion.2), channel_id=1, source_target_pairs={{0,128},{32,160},{64,192},{96,224},{128,0},{160,32},{192,64},{224,... | collective-permute-start | bytes 1572872 | tf_op jit(solution)/shard_map/ppermute | solution.py:37
  185.9 30.0 %collective-permute-done.9 = f32[2,256,256]{2,1,0:T(8,128)S(1)} collective-permute-done((f32[2,256,256]{2,1,0:T(8,128)S(1)}, f32[2,256,256]{2,1,0:T(8,128)S(1)}, u32[]{:S(2)}, u32[]{:S(2)}) %collective-permute-start.9) | collective-permute-done | bytes 524320 | tf_op jit(solution)/shard_map/ppermute | solution.py:26
  215.9 0.9 add_bitcast_fusion
  216.8 0.0 collective-permute-done.4
  216.8 0.9 fusion.2
  (2 shorter events, 0.1 us)
Async XLA Ops:
  0.6 6.1 %copy-start.1 = (s32[16,2]{0,1:T(2,128)S(1)}, s32[16,2]{0,1:T(2,128)}, u32[]{:S(2)}) copy-start(s32[16,2]{0,1:T(2,128)} %param.8) | copy-start | bytes 388
  2.4 25.5 %collective-permute-start = (f32[2,256,1024]{2,1,0:T(8,128)S(1)}, f32[2,256,1024]{2,1,0:T(8,128)}, u32[]{:S(2)}, u32[]{:S(2)}) collective-permute-start(f32[2,256,1024]{2,1,0:T(8,128)S(1)} %slice.35), channel_id=1, source_target_pairs={{1,0},{2,1},{3,2},{4,3},{5,4},{6,5},{7,6},{8,7},{9,8},{10,9},{11,1... | collective-permute-start | bytes 6291464 | tf_op jit(solution)/shard_map/ppermute | solution.py:17
  72.8 27.4 %collective-permute-start.1 = (f32[8,2,256,128]{3,2,1,0:T(8,128)S(1)}, f32[8,2,256,128]{3,2,1,0:T(8,128)S(1)}, u32[]{:S(2)}, u32[]{:S(2)}) collective-permute-start(f32[8,2,256,128]{3,2,1,0:T(8,128)S(1)} %slice.37), channel_id=1, source_target_pairs={{0,1},{1,2},{2,3},{3,4},{4,5},{5,6},{6,7},{7,8},{8,9},{9,10},{10,1... | collective-permute-start | bytes 6291464 | tf_op jit(solution)/shard_map/ppermute | solution.py:17
  103.2 1.7 copy-start
  103.3 48.3 %collective-permute-start.2 = (f32[2,2,2,512,128]{4,3,2,0,1:T(8,128)S(1)}, f32[2,2,2,512,128]{4,3,2,0,1:T(8,128)S(1)}, u32[]{:S(2)}, u32[]{:S(2)}) collective-permute-start(f32[2,2,2,512,128]{4,3,2,0,1:T(8,128)S(1)} %bitcast.51), channel_id=1, source_target_pairs={{0,32},{32,0},{64,96},{96,64},{128,160},{160,128},{192,224},{224,1... | collective-permute-start | bytes 6291464 | tf_op jit(solution)/shard_map/ppermute | solution.py:37
  104.9 1.9 collective-permute-start.5
  106.9 14.3 %collective-permute-start.6 = (f32[2,256,256]{2,1,0:T(8,128)S(1)}, f32[2,256,256]{2,1,0:T(8,128)S(1)}, u32[]{:S(2)}, u32[]{:S(2)}) collective-permute-start(f32[2,256,256]{2,1,0:T(8,128)S(1)} %add.66), channel_id=1, source_target_pairs={{0,2},{1,3},{2,0},{3,1},{4,6},{5,7},{6,4},{7,5},{8,10},{9,11},{10,... | collective-permute-start | bytes 1572872 | tf_op jit(solution)/shard_map/ppermute | solution.py:26
  121.3 33.8 %collective-permute-start.7 = (f32[2,256,256]{2,1,0:T(8,128)S(1)}, f32[2,256,256]{2,1,0:T(8,128)S(1)}, u32[]{:S(2)}, u32[]{:S(2)}) collective-permute-start(f32[2,256,256]{2,1,0:T(8,128)S(1)} %add.67), channel_id=1, source_target_pairs={{0,4},{1,5},{2,6},{3,7},{4,0},{5,1},{6,2},{7,3},{8,12},{9,13},{10,... | collective-permute-start | bytes 1572872 | tf_op jit(solution)/shard_map/ppermute | solution.py:26
  152.0 26.5 %collective-permute-start.3 = (f32[2,2,512,128]{3,2,1,0:T(8,128)S(1)}, f32[2,2,512,128]{3,2,1,0:T(8,128)S(1)}, u32[]{:S(2)}, u32[]{:S(2)}) collective-permute-start(f32[2,2,512,128]{3,2,1,0:T(8,128)S(1)} %slice_bitcast_fusion), channel_id=1, source_target_pairs={{0,64},{32,96},{64,0},{96,32},{128,192},{160,224},{192,128},{224,1... | collective-permute-start | bytes 3145736 | tf_op jit(solution)/shard_map/ppermute | solution.py:37
  155.2 13.5 %collective-permute-start.8 = (f32[2,256,256]{2,1,0:T(8,128)S(1)}, f32[2,256,256]{2,1,0:T(8,128)S(1)}, u32[]{:S(2)}, u32[]{:S(2)}) collective-permute-start(f32[2,256,256]{2,1,0:T(8,128)S(1)} %add.68), channel_id=1, source_target_pairs={{0,8},{1,9},{2,10},{3,11},{4,12},{5,13},{6,14},{7,15},{8,0},{9,1},... | collective-permute-start | bytes 1572872 | tf_op jit(solution)/shard_map/ppermute | solution.py:26
  168.7 47.2 %collective-permute-start.9 = (f32[2,256,256]{2,1,0:T(8,128)S(1)}, f32[2,256,256]{2,1,0:T(8,128)S(1)}, u32[]{:S(2)}, u32[]{:S(2)}) collective-permute-start(f32[2,256,256]{2,1,0:T(8,128)S(1)} %add.69), channel_id=1, source_target_pairs={{0,16},{1,17},{2,18},{3,19},{4,20},{5,21},{6,22},{7,23},{8,24},{9,... | collective-permute-start | bytes 1572872 | tf_op jit(solution)/shard_map/ppermute | solution.py:26
  178.6 38.2 %collective-permute-start.4 = (f32[2,512,128]{2,1,0:T(8,128)S(1)}, f32[2,512,128]{2,1,0:T(8,128)S(1)}, u32[]{:S(2)}, u32[]{:S(2)}) collective-permute-start(f32[2,512,128]{2,1,0:T(8,128)S(1)} %slice_bitcast_fusion.2), channel_id=1, source_target_pairs={{0,128},{32,160},{64,192},{96,224},{128,0},{160,32},{192,64},{224,... | collective-permute-start | bytes 1572872 | tf_op jit(solution)/shard_map/ppermute | solution.py:37
where the time goes:
time: 218 us
  waiting for transfers between devices  139 us (64%)
  Pallas kernels  36.7 us (17%)
  starting transfers between devices  22.2 us (10%)
  other arithmetic  14.7 us (7%)
  local copies, waits for them, and re-layouts  4.01 us (2%)
    ppermute x5, waiting for transfers between devices, sum_over(): block = block + lax.ppermute(block, axis, xor_route(axis, bit))  59.1 us
    ppermute x2, waiting for transfers between devices, from_behind(): return lax.ppermute(block, axis, route)  42.2 us
    ppermute x3, waiting for transfers between devices, sum_scatter_blocks(): held = kept + lax.ppermute(sent, axis, xor_route(axis, bit))  37.4 us
    pallas_call x1, Pallas kernels, fused_step(): pl.pallas_call(fused_kernel, grid_spec=grid_spec, out_shape=(jax.ShapeDty...  36.7 us
    ppermute x3, starting transfers between devices, sum_scatter_blocks(): held = kept + lax.ppermute(sent, axis, xor_route(axis, bit))  12 us
    ppermute x2, starting transfers between devices, from_behind(): return lax.ppermute(block, axis, route)  6.98 us
    concatenate x1, other arithmetic, on_device(): extended = jnp.concatenate([object_field, rim_rows], axis=1)  6.6 us
  transfers between devices with their start and end apart: 10, of which 8 were waited for; matrix products, arithmetic and copies ran while one was open for 2% of the time, Pallas kernels for 0%

commit v1 on v0

--- a/solution.py
+++ b/solution.py
@@ -21,8 +21,8 @@
     return [(i, i ^ (1 << bit)) for i in range(lax.axis_size(axis))]
 
 
-def sum_over(block, axis):
-    for bit in range(lax.axis_size(axis).bit_length() - 1):
+def sum_over(block, axis, order):
+    for bit in order:
         block = block + lax.ppermute(block, axis, xor_route(axis, bit))
     return block
 
@@ -256,12 +256,11 @@
         extended, probes[0], patterns[0], cos_table, sin_table, base, down, start, shift, place,
         counts, blocks, tile_rows + patch_side,
     )
-    probe_total = sum_over(probe_part, "region")
+    probe_total = sum_over(probe_part, "region", (3, 4, 0, 1, 2))
     arrived = from_behind(grad_ext[:, :, tile_rows:, :], "region", 1)
-    tile_grad = grad_ext[:, :, :tile_rows, :] + jnp.pad(
-        arrived, ((0, 0), (0, 0), (0, tile_rows - patch_side), (0, 0))
-    )
-    object_out = sum_scatter_blocks(tile_grad, "wave")
+    lower_out = sum_scatter_blocks(grad_ext[:, :, patch_side:tile_rows, :], "wave")
+    upper_out = sum_scatter_blocks(grad_ext[:, :, :patch_side, :] + arrived, "wave")
+    object_out = jnp.concatenate([upper_out, lower_out], axis=1)
     return (object_out, probe_total[None])
 
 

time: 218 us -> 201 us (0.922)
  the two profiles are of different devices: /device:TPU:8 before, /device:TPU:57 now
where the time goes in v1:
time: 201 us; the launch traced here: 197 us
  waiting for transfers between devices  123 us (61%)
  Pallas kernels  28.4 us (14%)
  starting transfers between devices  25.1 us (12%)
  other arithmetic  14.7 us (7%)
  local copies, waits for them, and re-layouts  4.07 us (2%)
    ppermute x6, waiting for transfers between devices, sum_scatter_blocks(): held = kept + lax.ppermute(sent, axis, xor_route(axis, bit))  56.2 us
    ppermute x5, waiting for transfers between devices, sum_over(): block = block + lax.ppermute(block, axis, xor_route(axis, bit))  43.9 us
    pallas_call x1, Pallas kernels, fused_step(): pl.pallas_call(fused_kernel, grid_spec=grid_spec, out_shape=(jax.ShapeDty...  28.4 us
    ppermute x2, waiting for transfers between devices, from_behind(): return lax.ppermute(block, axis, route)  23.3 us
    ppermute x6, starting transfers between devices, sum_scatter_blocks(): held = kept + lax.ppermute(sent, axis, xor_route(axis, bit))  20.2 us
    concatenate x1, other arithmetic, on_device(): extended = jnp.concatenate([object_field, rim_rows], axis=1)  6.62 us
    ppermute x2, starting transfers between devices, from_behind(): return lax.ppermute(block, axis, route)  4.51 us
  transfers between devices with their start and end apart: 13, of which 9 were waited for; matrix products, arithmetic and copies ran while one was open for 4% of the time, Pallas kernels for 0%

profile of v1, /device:TPU:57, one launch (start us, length us, event | category | flops | bytes accessed | tf_op | source)
XLA Modules:
  0.0 197.3 jit_solution(4064554363180801673)
XLA Ops:
  0.6 1.7 slice.56
  2.4 2.6 %collective-permute-start = (f32[2,256,1024]{2,1,0:T(8,128)S(1)}, f32[2,256,1024]{2,1,0:T(8,128)}, u32[]{:S(2)}, u32[]{:S(2)}) collective-permute-start(f32[2,256,1024]{2,1,0:T(8,128)S(1)} %slice.56), channel_id=1, source_target_pairs={{1,0},{2,1},{3,2},{4,3},{5,4},{6,5},{7,6},{8,7},{9,8},{10,9},{11,1... | collective-permute-start | bytes 6291464 | tf_op jit(solution)/shard_map/ppermute | solution.py:17
  5.6 1.7 multiply_convert_fusion
  7.4 0.6 bitcast_subtract_fusion
  8.0 0.7 add_xor_fusion.place_ref
  8.6 23.3 %collective-permute-done = f32[2,256,1024]{2,1,0:T(8,128)} collective-permute-done((f32[2,256,1024]{2,1,0:T(8,128)S(1)}, f32[2,256,1024]{2,1,0:T(8,128)}, u32[]{:S(2)}, u32[]{:S(2)}) %collective-permute-start) | collective-permute-done | bytes 2097184 | tf_op jit(solution)/shard_map/ppermute | solution.py:17
  31.9 6.6 %pad_maximum_fusion.ext_ref = f32[2,768,1024]{2,1,0:T(8,128)} fusion(f32[2,256,1024]{2,1,0:T(8,128)} %collective-permute-done, f32[2,512,1024]{2,1,0:T(8,128)} %param.5), kind=kLoop, calls=%fused_computation | loop fusion | flops 1572864 | bytes 12582912 | tf_op jit(solution)/shard_map/concatenate | solution.py:246
  38.6 28.4 %shard_map.68 = (f32[8,2,768,128]{3,2,1,0:T(8,128)}, f32[2,256,256]{2,1,0:T(8,128)}) custom-call(s32[16]{0:T(128)} %get-tuple-element.17.base_ref, s32[16]{0:T(128)} %get-tuple-element.16.down_ref, s32[16]{0:T(128)} %get-tuple-element.7.start_ref, s32[16]{0:T(128)} %get-tuple-element.6.shift_ref, s32[16,3]{1,0:T(8,128)} %add_xor_fusion.place_ref, ...), custom_call_target="tpu_custom_call" | custom-call | tf_op jit(solution)/shard_map/pallas_call | solution.py:209
  67.0 1.8 slice.58
  68.8 1.9 collective-permute-start.1
  70.7 0.1 collective-permute-start.8
  70.8 36.8 %collective-permute-done.8 = f32[2,256,256]{2,1,0:T(8,128)S(1)} collective-permute-done((f32[2,256,256]{2,1,0:T(8,128)S(1)}, f32[2,256,256]{2,1,0:T(8,128)S(1)}, u32[]{:S(2)}, u32[]{:S(2)}) %collective-permute-start.8) | collective-permute-done | bytes 524320 | tf_op jit(solution)/shard_map/ppermute | solution.py:26
  107.6 0.1 add.76
  107.7 0.1 collective-permute-start.9
  107.8 0.0 collective-permute-done.1
  107.8 2.7 %slice_add_fusion = (f32[8,2,256,128]{3,2,1,0:T(8,128)S(1)}, f32[8,2,256,128]{3,2,1,0:T(8,128)S(1)}) fusion(f32[8,2,256,128]{3,2,1,0:T(8,128)S(1)} %collective-permute-done.1, f32[8,2,768,128]{3,2,1,0:T(8,128)} %get-tuple-element.4), kind=kLoop, calls=%fused_computation.1 | loop fusion | flops 524288 | bytes 10485760 | tf_op jit(solution)/shard_map/add | solution.py:262
  110.5 0.1 fusion.16
  110.6 0.1 copy.23
  110.7 1.3 collective-permute-start.5
  112.0 6.8 %collective-permute-done.9 = f32[2,256,256]{2,1,0:T(8,128)S(1)} collective-permute-done((f32[2,256,256]{2,1,0:T(8,128)S(1)}, f32[2,256,256]{2,1,0:T(8,128)S(1)}, u32[]{:S(2)}, u32[]{:S(2)}) %collective-permute-start.9) | collective-permute-done | bytes 524320 | tf_op jit(solution)/shard_map/ppermute | solution.py:26
  118.8 0.1 add.77
  118.9 0.1 collective-permute-start.10
  119.0 0.1 fusion.15
  119.1 0.1 copy.24
  119.2 1.3 collective-permute-start.2
  120.5 0.4 collective-permute-done.10
  120.9 0.1 add.78
  120.9 0.1 collective-permute-start.11
  121.0 14.9 %collective-permute-done.5 = f32[2,2,2,256,128]{4,3,2,0,1:T(8,128)S(1)} collective-permute-done((f32[2,2,2,256,128]{4,3,2,0,1:T(8,128)S(1)}, f32[2,2,2,256,128]{4,3,2,0,1:T(8,128)S(1)}, u32[]{:S(2)}, u32[]{:S(2)}) %collective-permute-start.5) | collective-permute-done | bytes 1048608 | tf_op jit(solution)/shard_map/ppermute | solution.py:37
  136.0 0.1 fusion
  136.1 2.8 %collective-permute-start.6 = (f32[2,2,256,128]{3,2,1,0:T(8,128)S(1)}, f32[2,2,256,128]{3,2,1,0:T(8,128)S(1)}, u32[]{:S(2)}, u32[]{:S(2)}) collective-permute-start(f32[2,2,256,128]{3,2,1,0:T(8,128)S(1)} %slice_bitcast_fusion), channel_id=1, source_target_pairs={{0,64},{32,96},{64,0},{96,32},{128,192},{160,224},{192,128},{224,1... | collective-permute-start | bytes 1572872 | tf_op jit(solution)/shard_map/ppermute | solution.py:37
  138.9 19.5 %collective-permute-done.2 = f32[2,2,2,256,128]{4,3,2,0,1:T(8,128)S(1)} collective-permute-done((f32[2,2,2,256,128]{4,3,2,0,1:T(8,128)S(1)}, f32[2,2,2,256,128]{4,3,2,0,1:T(8,128)S(1)}, u32[]{:S(2)}, u32[]{:S(2)}) %collective-permute-start.2) | collective-permute-done | bytes 1048608 | tf_op jit(solution)/shard_map/ppermute | solution.py:37
  158.4 0.1 fusion.1
  158.6 2.8 %collective-permute-start.3 = (f32[2,2,256,128]{3,2,1,0:T(8,128)S(1)}, f32[2,2,256,128]{3,2,1,0:T(8,128)S(1)}, u32[]{:S(2)}, u32[]{:S(2)}) collective-permute-start(f32[2,2,256,128]{3,2,1,0:T(8,128)S(1)} %slice_bitcast_fusion.2), channel_id=1, source_target_pairs={{0,64},{32,96},{64,0},{96,32},{128,192},{160,224},{192,128},{224,1... | collective-permute-start | bytes 1572872 | tf_op jit(solution)/shard_map/ppermute | solution.py:37
  161.4 0.0 collective-permute-done.11
  161.4 0.1 add.79
  161.5 0.1 collective-permute-start.12
  161.6 10.3 %collective-permute-done.6 = f32[2,2,256,128]{3,2,1,0:T(8,128)S(1)} collective-permute-done((f32[2,2,256,128]{3,2,1,0:T(8,128)S(1)}, f32[2,2,256,128]{3,2,1,0:T(8,128)S(1)}, u32[]{:S(2)}, u32[]{:S(2)}) %collective-permute-start.6) | collective-permute-done | bytes 524320 | tf_op jit(solution)/shard_map/ppermute | solution.py:37
  171.9 0.1 fusion.2
  171.9 6.7 %collective-permute-start.7 = (f32[2,256,128]{2,1,0:T(8,128)S(1)}, f32[2,256,128]{2,1,0:T(8,128)S(1)}, u32[]{:S(2)}, u32[]{:S(2)}) collective-permute-start(f32[2,256,128]{2,1,0:T(8,128)S(1)} %slice_bitcast_fusion.4), channel_id=1, source_target_pairs={{0,128},{32,160},{64,192},{96,224},{128,0},{160,32},{192,64},{224,... | collective-permute-start | bytes 786440 | tf_op jit(solution)/shard_map/ppermute | solution.py:37
  178.6 0.0 collective-permute-done.3
  178.6 0.1 fusion.3
  178.7 5.2 %collective-permute-start.4 = (f32[2,256,128]{2,1,0:T(8,128)S(1)}, f32[2,256,128]{2,1,0:T(8,128)S(1)}, u32[]{:S(2)}, u32[]{:S(2)}) collective-permute-start(f32[2,256,128]{2,1,0:T(8,128)S(1)} %slice_bitcast_fusion.6), channel_id=1, source_target_pairs={{0,128},{32,160},{64,192},{96,224},{128,0},{160,32},{192,64},{224,... | collective-permute-start | bytes 786440 | tf_op jit(solution)/shard_map/ppermute | solution.py:37
  184.0 0.0 collective-permute-done.12
  184.0 0.9 add_bitcast_fusion
  184.8 8.2 %collective-permute-done.7 = f32[2,256,128]{2,1,0:T(8,128)S(1)} collective-permute-done((f32[2,256,128]{2,1,0:T(8,128)S(1)}, f32[2,256,128]{2,1,0:T(8,128)S(1)}, u32[]{:S(2)}, u32[]{:S(2)}) %collective-permute-start.7) | collective-permute-done | bytes 262176 | tf_op jit(solution)/shard_map/ppermute | solution.py:37
  193.1 3.3 %collective-permute-done.4 = f32[2,256,128]{2,1,0:T(8,128)S(1)} collective-permute-done((f32[2,256,128]{2,1,0:T(8,128)S(1)}, f32[2,256,128]{2,1,0:T(8,128)S(1)}, u32[]{:S(2)}, u32[]{:S(2)}) %collective-permute-start.4) | collective-permute-done | bytes 262176 | tf_op jit(solution)/shard_map/ppermute | solution.py:37
  196.5 0.8 pad_maximum_fusion.1
  (11 shorter events, 0.2 us)
Async XLA Ops:
  0.6 6.7 %copy-start.1 = (s32[16,2]{0,1:T(2,128)S(1)}, s32[16,2]{0,1:T(2,128)}, u32[]{:S(2)}) copy-start(s32[16,2]{0,1:T(2,128)} %param.8) | copy-start | bytes 388
  2.4 29.6 %collective-permute-start = (f32[2,256,1024]{2,1,0:T(8,128)S(1)}, f32[2,256,1024]{2,1,0:T(8,128)}, u32[]{:S(2)}, u32[]{:S(2)}) collective-permute-start(f32[2,256,1024]{2,1,0:T(8,128)S(1)} %slice.56), channel_id=1, source_target_pairs={{1,0},{2,1},{3,2},{4,3},{5,4},{6,5},{7,6},{8,7},{9,8},{10,9},{11,1... | collective-permute-start | bytes 6291464 | tf_op jit(solution)/shard_map/ppermute | solution.py:17
  67.0 3.7 %copy-start = (f32[2,256,256]{2,1,0:T(8,128)S(1)}, f32[2,256,256]{2,1,0:T(8,128)}, u32[]{:S(2)}) copy-start(f32[2,256,256]{2,1,0:T(8,128)} %get-tuple-element.5) | copy-start | bytes 1572868
  68.8 39.0 %collective-permute-start.1 = (f32[8,2,256,128]{3,2,1,0:T(8,128)S(1)}, f32[8,2,256,128]{3,2,1,0:T(8,128)S(1)}, u32[]{:S(2)}, u32[]{:S(2)}) collective-permute-start(f32[8,2,256,128]{3,2,1,0:T(8,128)S(1)} %slice.58), channel_id=1, source_target_pairs={{0,1},{1,2},{2,3},{3,4},{4,5},{5,6},{6,7},{7,8},{8,9},{9,10},{10,1... | collective-permute-start | bytes 6291464 | tf_op jit(solution)/shard_map/ppermute | solution.py:17
  70.7 36.9 %collective-permute-start.8 = (f32[2,256,256]{2,1,0:T(8,128)S(1)}, f32[2,256,256]{2,1,0:T(8,128)S(1)}, u32[]{:S(2)}, u32[]{:S(2)}) collective-permute-start(f32[2,256,256]{2,1,0:T(8,128)S(1)} %copy-done), channel_id=1, source_target_pairs={{0,8},{1,9},{2,10},{3,11},{4,12},{5,13},{6,14},{7,15},{8,0},{9,1},... | collective-permute-start | bytes 1572872 | tf_op jit(solution)/shard_map/ppermute | solution.py:26
  107.7 11.1 %collective-permute-start.9 = (f32[2,256,256]{2,1,0:T(8,128)S(1)}, f32[2,256,256]{2,1,0:T(8,128)S(1)}, u32[]{:S(2)}, u32[]{:S(2)}) collective-permute-start(f32[2,256,256]{2,1,0:T(8,128)S(1)} %add.76), channel_id=1, source_target_pairs={{0,16},{1,17},{2,18},{3,19},{4,20},{5,21},{6,22},{7,23},{8,24},{9,... | collective-permute-start | bytes 1572872 | tf_op jit(solution)/shard_map/ppermute | solution.py:26
  110.7 25.3 %collective-permute-start.5 = (f32[2,2,2,256,128]{4,3,2,0,1:T(8,128)S(1)}, f32[2,2,2,256,128]{4,3,2,0,1:T(8,128)S(1)}, u32[]{:S(2)}, u32[]{:S(2)}) collective-permute-start(f32[2,2,2,256,128]{4,3,2,0,1:T(8,128)S(1)} %bitcast.73), channel_id=1, source_target_pairs={{0,32},{32,0},{64,96},{96,64},{128,160},{160,128},{192,224},{224,1... | collective-permute-start | bytes 3145736 | tf_op jit(solution)/shard_map/ppermute | solution.py:37
  118.9 2.0 %collective-permute-start.10 = (f32[2,256,256]{2,1,0:T(8,128)S(1)}, f32[2,256,256]{2,1,0:T(8,128)S(1)}, u32[]{:S(2)}, u32[]{:S(2)}) collective-permute-start(f32[2,256,256]{2,1,0:T(8,128)S(1)} %add.77), channel_id=1, source_target_pairs={{0,1},{1,0},{2,3},{3,2},{4,5},{5,4},{6,7},{7,6},{8,9},{9,8},{10,11... | collective-permute-start | bytes 1572872 | tf_op jit(solution)/shard_map/ppermute | solution.py:26
  119.2 39.3 %collective-permute-start.2 = (f32[2,2,2,256,128]{4,3,2,0,1:T(8,128)S(1)}, f32[2,2,2,256,128]{4,3,2,0,1:T(8,128)S(1)}, u32[]{:S(2)}, u32[]{:S(2)}) collective-permute-start(f32[2,2,2,256,128]{4,3,2,0,1:T(8,128)S(1)} %bitcast.74), channel_id=1, source_target_pairs={{0,32},{32,0},{64,96},{96,64},{128,160},{160,128},{192,224},{224,1... | collective-permute-start | bytes 3145736 | tf_op jit(solution)/shard_map/ppermute | solution.py:37
  120.9 40.5 %collective-permute-start.11 = (f32[2,256,256]{2,1,0:T(8,128)S(1)}, f32[2,256,256]{2,1,0:T(8,128)S(1)}, u32[]{:S(2)}, u32[]{:S(2)}) collective-permute-start(f32[2,256,256]{2,1,0:T(8,128)S(1)} %add.78), channel_id=1, source_target_pairs={{0,2},{1,3},{2,0},{3,1},{4,6},{5,7},{6,4},{7,5},{8,10},{9,11},{10,... | collective-permute-start | bytes 1572872 | tf_op jit(solution)/shard_map/ppermute | solution.py:26
  136.1 35.7 %collective-permute-start.6 = (f32[2,2,256,128]{3,2,1,0:T(8,128)S(1)}, f32[2,2,256,128]{3,2,1,0:T(8,128)S(1)}, u32[]{:S(2)}, u32[]{:S(2)}) collective-permute-start(f32[2,2,256,128]{3,2,1,0:T(8,128)S(1)} %slice_bitcast_fusion), channel_id=1, source_target_pairs={{0,64},{32,96},{64,0},{96,32},{128,192},{160,224},{192,128},{224,1... | collective-permute-start | bytes 1572872 | tf_op jit(solution)/shard_map/ppermute | solution.py:37
  158.6 20.0 %collective-permute-start.3 = (f32[2,2,256,128]{3,2,1,0:T(8,128)S(1)}, f32[2,2,256,128]{3,2,1,0:T(8,128)S(1)}, u32[]{:S(2)}, u32[]{:S(2)}) collective-permute-start(f32[2,2,256,128]{3,2,1,0:T(8,128)S(1)} %slice_bitcast_fusion.2), channel_id=1, source_target_pairs={{0,64},{32,96},{64,0},{96,32},{128,192},{160,224},{192,128},{224,1... | collective-permute-start | bytes 1572872 | tf_op jit(solution)/shard_map/ppermute | solution.py:37
  161.5 22.5 %collective-permute-start.12 = (f32[2,256,256]{2,1,0:T(8,128)S(1)}, f32[2,256,256]{2,1,0:T(8,128)S(1)}, u32[]{:S(2)}, u32[]{:S(2)}) collective-permute-start(f32[2,256,256]{2,1,0:T(8,128)S(1)} %add.79), channel_id=1, source_target_pairs={{0,4},{1,5},{2,6},{3,7},{4,0},{5,1},{6,2},{7,3},{8,12},{9,13},{10,... | collective-permute-start | bytes 1572872 | tf_op jit(solution)/shard_map/ppermute | solution.py:26
  171.9 21.1 %collective-permute-start.7 = (f32[2,256,128]{2,1,0:T(8,128)S(1)}, f32[2,256,128]{2,1,0:T(8,128)S(1)}, u32[]{:S(2)}, u32[]{:S(2)}) collective-permute-start(f32[2,256,128]{2,1,0:T(8,128)S(1)} %slice_bitcast_fusion.4), channel_id=1, source_target_pairs={{0,128},{32,160},{64,192},{96,224},{128,0},{160,32},{192,64},{224,... | collective-permute-start | bytes 786440 | tf_op jit(solution)/shard_map/ppermute | solution.py:37
  178.7 17.7 %collective-permute-start.4 = (f32[2,256,128]{2,1,0:T(8,128)S(1)}, f32[2,256,128]{2,1,0:T(8,128)S(1)}, u32[]{:S(2)}, u32[]{:S(2)}) collective-permute-start(f32[2,256,128]{2,1,0:T(8,128)S(1)} %slice_bitcast_fusion.6), channel_id=1, source_target_pairs={{0,128},{32,160},{64,192},{96,224},{128,0},{160,32},{192,64},{224,... | collective-permute-start | bytes 786440 | tf_op jit(solution)/shard_map/ppermute | solution.py:37

commit v2 on v0

--- a/solution.py
+++ b/solution.py
@@ -21,8 +21,8 @@
     return [(i, i ^ (1 << bit)) for i in range(lax.axis_size(axis))]
 
 
-def sum_over(block, axis):
-    for bit in range(lax.axis_size(axis).bit_length() - 1):
+def sum_over(block, axis, order):
+    for bit in order:
         block = block + lax.ppermute(block, axis, xor_route(axis, bit))
     return block
 
@@ -122,18 +122,26 @@
 
 
 def fused_kernel(base_ref, down_ref, start_ref, shift_ref, place_ref, count_ref,
-                 ext_ref, probe_ref, pattern_ref, cos_ref, sin_ref, grad_ref, prb_ref, pad_ref):
+                 tile_ref, rim_ref, probe_ref, pattern_ref, fwd_ref, bwd_ref,
+                 grad_ref, prb_ref, ext_ref, pad_ref, sems):
     s = pl.program_id(0)
     side = probe_ref.shape[-1]
+    tile_rows = tile_ref.shape[1]
     high = side + SUB
     wide = side + LANE
     spans = place_ref.shape[1]
 
     @pl.when(s == 0)
     def _():
+        own = pltpu.make_async_copy(tile_ref, ext_ref.at[:, :tile_rows, :], sems.at[0])
+        rim = pltpu.make_async_copy(rim_ref, ext_ref.at[:, tile_rows:, :], sems.at[1])
+        own.start()
+        rim.start()
         grad_ref[...] = jnp.zeros_like(grad_ref)
         prb_ref[...] = jnp.zeros_like(prb_ref)
         pad_ref[...] = jnp.zeros_like(pad_ref)
+        own.wait()
+        rim.wait()
 
     @pl.when(s < count_ref[0])
     def _():
@@ -152,28 +160,27 @@
         x_re, x_im = cut
         p_re = probe_ref[0]
         p_im = probe_ref[1]
-        cos_t = cos_ref[...]
-        sin_t = sin_ref[...]
-
-        def left_mul(table, part):
-            return jnp.dot(table, part, preferred_element_type=jnp.float32)
-
-        def right_mul(part, table):
-            return jnp.dot(part, table, preferred_element_type=jnp.float32)
-
-        wave_re = (p_re * x_re - p_im * x_im).astype(jnp.bfloat16)
-        wave_im = (p_re * x_im + p_im * x_re).astype(jnp.bfloat16)
-        half_re = (left_mul(cos_t, wave_re) + left_mul(sin_t, wave_im)).astype(jnp.bfloat16)
-        half_im = (left_mul(cos_t, wave_im) - left_mul(sin_t, wave_re)).astype(jnp.bfloat16)
-        far_re = right_mul(half_re, cos_t) + right_mul(half_im, sin_t)
-        far_im = right_mul(half_im, cos_t) - right_mul(half_re, sin_t)
+        fwd = fwd_ref[...]
+        bwd = bwd_ref[...]
+
+        def dot(a, b):
+            return jnp.dot(a, b, preferred_element_type=jnp.float32)
+
+        wave = jnp.concatenate(
+            [(p_re * x_re - p_im * x_im).astype(jnp.bfloat16),
+             (p_re * x_im + p_im * x_re).astype(jnp.bfloat16)], axis=0)
+        half = dot(fwd, wave).astype(jnp.bfloat16)
+        far = dot(jnp.concatenate([half[:side], half[side:]], axis=1), bwd)
+        far_re = far[:, :side]
+        far_im = far[:, side:]
         excess = far_re * far_re + far_im * far_im - pattern_ref[0].astype(jnp.float32)
-        back_re = (excess * far_re).astype(jnp.bfloat16)
-        back_im = (excess * far_im).astype(jnp.bfloat16)
-        inner_re = (left_mul(cos_t, back_re) - left_mul(sin_t, back_im)).astype(jnp.bfloat16)
-        inner_im = (left_mul(cos_t, back_im) + left_mul(sin_t, back_re)).astype(jnp.bfloat16)
-        chi_re = right_mul(inner_re, cos_t) - right_mul(inner_im, sin_t)
-        chi_im = right_mul(inner_im, cos_t) + right_mul(inner_re, sin_t)
+        back = jnp.concatenate(
+            [(excess * far_re).astype(jnp.bfloat16), (excess * far_im).astype(jnp.bfloat16)],
+            axis=0)
+        inner = dot(bwd, back).astype(jnp.bfloat16)
+        chi = dot(jnp.concatenate([inner[:side], inner[side:]], axis=1), fwd)
+        chi_re = chi[:, :side]
+        chi_im = chi[:, side:]
         prb_ref[0] += x_re * chi_re + x_im * chi_im
         prb_ref[1] += x_re * chi_im - x_im * chi_re
         terms = (p_re * chi_re + p_im * chi_im, p_re * chi_im - p_im * chi_re)
@@ -185,26 +192,32 @@
                 grad_ref[place_ref[s, k], c, pl.ds(base, high), :] += term[:, k * LANE:(k + 1) * LANE]
 
 
-def fused_step(extended, probe, patterns, cos_table, sin_table, base, down, start, shift, place,
-               count, blocks, rows_out):
+def fused_step(tile, rim, probe, patterns, fwd, bwd, base, down, start, shift, place,
+               count, blocks):
     slots, side, _ = patterns.shape
+    rows_out = tile.shape[1] + rim.shape[1]
     whole2 = lambda s, *_: (0, 0)
     whole3 = lambda s, *_: (0, 0, 0)
     grid_spec = pltpu.PrefetchScalarGridSpec(
         num_scalar_prefetch=6,
         grid=(slots,),
         in_specs=[
-            pl.BlockSpec(extended.shape, whole3),
+            pl.BlockSpec(memory_space=pl.ANY),
+            pl.BlockSpec(memory_space=pl.ANY),
             pl.BlockSpec(probe.shape, whole3),
             pl.BlockSpec((1, side, side), lambda s, *_: (s, 0, 0)),
-            pl.BlockSpec(cos_table.shape, whole2),
-            pl.BlockSpec(sin_table.shape, whole2),
+            pl.BlockSpec(fwd.shape, whole2),
+            pl.BlockSpec(bwd.shape, whole2),
         ],
         out_specs=[
             pl.BlockSpec((blocks, 2, rows_out, LANE), lambda s, *_: (0, 0, 0, 0)),
             pl.BlockSpec(probe.shape, whole3),
         ],
-        scratch_shapes=[pltpu.VMEM((side + SUB, side + LANE), jnp.float32)],
+        scratch_shapes=[
+            pltpu.VMEM((2, rows_out, tile.shape[2]), jnp.float32),
+            pltpu.VMEM((side + SUB, side + LANE), jnp.float32),
+            pltpu.SemaphoreType.DMA((2,)),
+        ],
     )
     return pl.pallas_call(
         fused_kernel,
@@ -214,7 +227,17 @@
             jax.ShapeDtypeStruct(probe.shape, jnp.float32),
         ),
         compiler_params=pltpu.CompilerParams(vmem_limit_bytes=60 * 1024 * 1024),
-    )(base, down, start, shift, place, count, extended, probe, patterns, cos_table, sin_table)
+    )(base, down, start, shift, place, count, tile, rim, probe, patterns, fwd, bwd)
+
+
+def stacked_tables(cos_table, sin_table):
+    fwd = jnp.concatenate(
+        [jnp.concatenate([cos_table, sin_table], axis=1),
+         jnp.concatenate([-sin_table, cos_table], axis=1)], axis=0)
+    bwd = jnp.concatenate(
+        [jnp.concatenate([cos_table, -sin_table], axis=1),
+         jnp.concatenate([sin_table, cos_table], axis=1)], axis=0)
+    return fwd, bwd
 
 
 def make_tables(patch_side):
@@ -243,7 +266,6 @@
     slot_total = offsets.shape[0]
     top_rows = object_field[:, :patch_side, :]
     rim_rows = from_behind(top_rows, "region", -1)
-    extended = jnp.concatenate([object_field, rim_rows], axis=1)
     base, down, start, shift = windows(offsets, patch_side, width_cols)
     cos_table, sin_table = make_tables(patch_side)
     blocks = lax.axis_size("wave")
@@ -252,11 +274,12 @@
     place = jnp.bitwise_xor(
         first[:, None] + jnp.arange(spans, dtype=jnp.int32)[None, :], lax.axis_index("wave")
     ).astype(jnp.int32)
+    fwd, bwd = stacked_tables(cos_table, sin_table)
     grad_ext, probe_part = fused_step(
-        extended, probes[0], patterns[0], cos_table, sin_table, base, down, start, shift, place,
-        counts, blocks, tile_rows + patch_side,
-    )
-    probe_total = sum_over(probe_part, "region")
+        object_field, rim_rows, probes[0], patterns[0], fwd, bwd, base, down, start, shift,
+        place, counts, blocks,
+    )
+    probe_total = sum_over(probe_part, "region", (3, 4, 0, 1, 2))
     arrived = from_behind(grad_ext[:, :, tile_rows:, :], "region", 1)
     tile_grad = grad_ext[:, :, :tile_rows, :] + jnp.pad(
         arrived, ((0, 0), (0, 0), (0, tile_rows - patch_side), (0, 0))

time: 218 us -> 210 us (0.963)
  the two profiles are of different devices: /device:TPU:8 before, /device:TPU:25 now
where the time goes in v2:
time: 210 us
  waiting for transfers between devices  130 us (62%)
  Pallas kernels  36.9 us (18%)
  starting transfers between devices  24.8 us (12%)
  other arithmetic  9.56 us (5%)
  local copies, waits for them, and re-layouts  6.82 us (3%)
    ppermute x5, waiting for transfers between devices, sum_over(): block = block + lax.ppermute(block, axis, xor_route(axis, bit))  49.7 us
    ppermute x2, waiting for transfers between devices, from_behind(): return lax.ppermute(block, axis, route)  44.9 us
    pallas_call x1, Pallas kernels, fused_step(): pl.pallas_call(fused_kernel, grid_spec=grid_spec, out_shape=(jax.ShapeDty...  36.9 us
    ppermute x3, waiting for transfers between devices, sum_scatter_blocks(): held = kept + lax.ppermute(sent, axis, xor_route(axis, bit))  35.7 us
    ppermute x2, starting transfers between devices, from_behind(): return lax.ppermute(block, axis, route)  11.6 us
    ppermute x3, starting transfers between devices, sum_scatter_blocks(): held = kept + lax.ppermute(sent, axis, xor_route(axis, bit))  11.1 us
  transfers between devices with their start and end apart: 10, of which 8 were waited for; matrix products, arithmetic and copies ran while one was open for 3% of the time, Pallas kernels for 0%

profile of v2, /device:TPU:25, one launch (start us, length us, event | category | flops | bytes accessed | tf_op | source)
XLA Modules:
  0.0 209.8 jit_solution(12735102456937292725)
XLA Ops:
  0.6 0.0 copy-start.2
  0.6 3.2 %slice.35 = f32[2,256,1024]{2,1,0:T(8,128)} slice(f32[2,512,1024]{2,1,0:T(8,128)} %tile_ref.1), slice={[0:2], [0:256], [0:1024]} | slice | bytes 4194304 | tf_op jit(solution)/shard_map/slice | solution.py:267
  3.8 2.6 %collective-permute-start = (f32[2,256,1024]{2,1,0:T(8,128)}, f32[2,256,1024]{2,1,0:T(8,128)S(1)}, u32[]{:S(2)}, u32[]{:S(2)}) collective-permute-start(f32[2,256,1024]{2,1,0:T(8,128)} %slice.35), channel_id=1, source_target_pairs={{1,0},{2,1},{3,2},{4,3},{5,4},{6,5},{7,6},{8,7},{9,8},{10,9},{11,1... | collective-permute-start | bytes 6291464 | tf_op jit(solution)/shard_map/ppermute | solution.py:17
  7.1 1.0 fusion.11
  8.1 1.1 multiply_convert_fusion
  9.2 1.0 fusion.3
  10.2 0.0 copy-done.2
  10.2 0.6 bitcast_subtract_fusion
  10.8 0.7 add_xor_fusion.place_ref
  11.5 22.0 %collective-permute-done.rim_ref = f32[2,256,1024]{2,1,0:T(8,128)S(1)} collective-permute-done((f32[2,256,1024]{2,1,0:T(8,128)}, f32[2,256,1024]{2,1,0:T(8,128)S(1)}, u32[]{:S(2)}, u32[]{:S(2)}) %collective-permute-start) | collective-permute-done | bytes 2097184 | tf_op jit(solution)/shard_map/ppermute | solution.py:17
  33.5 0.0 copy-start
  33.5 1.3 copy-done
  34.8 36.9 %shard_map.68 = (f32[8,2,768,128]{3,2,1,0:T(8,128)}, f32[2,256,256]{2,1,0:T(8,128)}) custom-call(s32[16]{0:T(128)} %get-tuple-element.15.base_ref, s32[16]{0:T(128)} %get-tuple-element.14.down_ref, s32[16]{0:T(128)} %get-tuple-element.7.start_ref, s32[16]{0:T(128)} %get-tuple-element.6.shift_ref, s32[16,3]{1,0:T(8,128)} %add_xor_fusion.place_ref, ...), custom_call_target="tpu_custom_call" | custom-call | tf_op jit(solution)/shard_map/pallas_call | solution.py:222
  71.7 1.7 slice.37
  73.5 9.0 %collective-permute-start.1 = (f32[8,2,256,128]{3,2,1,0:T(8,128)S(1)}, f32[8,2,256,128]{3,2,1,0:T(8,128)S(1)}, u32[]{:S(2)}, u32[]{:S(2)}) collective-permute-start(f32[8,2,256,128]{3,2,1,0:T(8,128)S(1)} %slice.37), channel_id=1, source_target_pairs={{0,1},{1,2},{2,3},{3,4},{4,5},{5,6},{6,7},{7,8},{8,9},{9,10},{10,1... | collective-permute-start | bytes 6291464 | tf_op jit(solution)/shard_map/ppermute | solution.py:17
  82.5 23.0 %collective-permute-done.1 = f32[8,2,256,128]{3,2,1,0:T(8,128)S(1)} collective-permute-done((f32[8,2,256,128]{3,2,1,0:T(8,128)S(1)}, f32[8,2,256,128]{3,2,1,0:T(8,128)S(1)}, u32[]{:S(2)}, u32[]{:S(2)}) %collective-permute-start.1) | collective-permute-done | bytes 2097184 | tf_op jit(solution)/shard_map/ppermute | solution.py:17
  105.5 2.7 %pad_add_fusion = f32[8,2,512,128]{3,2,1,0:T(8,128)S(1)} fusion(f32[8,2,256,128]{3,2,1,0:T(8,128)S(1)} %collective-permute-done.1, f32[8,2,768,128]{3,2,1,0:T(8,128)} %get-tuple-element.4), kind=kLoop, calls=%fused_computation | loop fusion | flops 1048576 | bytes 10485760 | tf_op jit(solution)/shard_map/add | solution.py:284
  108.2 0.3 fusion.15
  108.5 0.0 copy-start.1
  108.5 0.1 copy.15
  108.6 1.3 collective-permute-start.2
  109.9 0.0 copy-done.1
  109.9 0.0 collective-permute-start.5
  109.9 11.9 %collective-permute-done.5 = f32[2,256,256]{2,1,0:T(8,128)S(1)} collective-permute-done((f32[2,256,256]{2,1,0:T(8,128)S(1)}, f32[2,256,256]{2,1,0:T(8,128)S(1)}, u32[]{:S(2)}, u32[]{:S(2)}) %collective-permute-start.5) | collective-permute-done | bytes 524320 | tf_op jit(solution)/shard_map/ppermute | solution.py:26
  121.8 0.1 add.78
  121.9 0.5 collective-permute-start.6
  122.4 24.7 %collective-permute-done.6 = f32[2,256,256]{2,1,0:T(8,128)S(1)} collective-permute-done((f32[2,256,256]{2,1,0:T(8,128)S(1)}, f32[2,256,256]{2,1,0:T(8,128)S(1)}, u32[]{:S(2)}, u32[]{:S(2)}) %collective-permute-start.6) | collective-permute-done | bytes 524320 | tf_op jit(solution)/shard_map/ppermute | solution.py:26
  147.1 0.1 add.79
  147.2 1.5 collective-permute-start.7
  148.6 5.1 %collective-permute-done.2 = f32[2,2,2,512,128]{4,3,2,0,1:T(8,128)S(1)} collective-permute-done((f32[2,2,2,512,128]{4,3,2,0,1:T(8,128)S(1)}, f32[2,2,2,512,128]{4,3,2,0,1:T(8,128)S(1)}, u32[]{:S(2)}, u32[]{:S(2)}) %collective-permute-start.2) | collective-permute-done | bytes 2097184 | tf_op jit(solution)/shard_map/ppermute | solution.py:37
  153.7 0.3 fusion
  154.0 0.1 slice_bitcast_fusion
  154.1 2.8 %collective-permute-start.3 = (f32[2,2,512,128]{3,2,1,0:T(8,128)S(1)}, f32[2,2,512,128]{3,2,1,0:T(8,128)S(1)}, u32[]{:S(2)}, u32[]{:S(2)}) collective-permute-start(f32[2,2,512,128]{3,2,1,0:T(8,128)S(1)} %slice_bitcast_fusion), channel_id=1, source_target_pairs={{0,64},{32,96},{64,0},{96,32},{128,192},{160,224},{192,128},{224,1... | collective-permute-start | bytes 3145736 | tf_op jit(solution)/shard_map/ppermute | solution.py:37
  156.9 0.0 collective-permute-done.7
  156.9 0.1 add.80
  157.0 0.1 collective-permute-start.8
  157.1 13.0 %collective-permute-done.8 = f32[2,256,256]{2,1,0:T(8,128)S(1)} collective-permute-done((f32[2,256,256]{2,1,0:T(8,128)S(1)}, f32[2,256,256]{2,1,0:T(8,128)S(1)}, u32[]{:S(2)}, u32[]{:S(2)}) %collective-permute-start.8) | collective-permute-done | bytes 524320 | tf_op jit(solution)/shard_map/ppermute | solution.py:26
  170.1 0.1 add.81
  170.2 0.1 collective-permute-start.9
  170.3 9.4 %collective-permute-done.3 = f32[2,2,512,128]{3,2,1,0:T(8,128)S(1)} collective-permute-done((f32[2,2,512,128]{3,2,1,0:T(8,128)S(1)}, f32[2,2,512,128]{3,2,1,0:T(8,128)S(1)}, u32[]{:S(2)}, u32[]{:S(2)}) %collective-permute-start.3) | collective-permute-done | bytes 1048608 | tf_op jit(solution)/shard_map/ppermute | solution.py:37
  179.7 0.1 fusion.1
  179.8 7.0 %collective-permute-start.4 = (f32[2,512,128]{2,1,0:T(8,128)S(1)}, f32[2,512,128]{2,1,0:T(8,128)S(1)}, u32[]{:S(2)}, u32[]{:S(2)}) collective-permute-start(f32[2,512,128]{2,1,0:T(8,128)S(1)} %slice_bitcast_fusion.2), channel_id=1, source_target_pairs={{0,128},{32,160},{64,192},{96,224},{128,0},{160,32},{192,64},{224,... | collective-permute-start | bytes 1572872 | tf_op jit(solution)/shard_map/ppermute | solution.py:37
  186.8 0.0 collective-permute-done.9
  186.8 0.9 add_bitcast_fusion
  187.7 21.3 %collective-permute-done.4 = f32[2,512,128]{2,1,0:T(8,128)S(1)} collective-permute-done((f32[2,512,128]{2,1,0:T(8,128)S(1)}, f32[2,512,128]{2,1,0:T(8,128)S(1)}, u32[]{:S(2)}, u32[]{:S(2)}) %collective-permute-start.4) | collective-permute-done | bytes 524320 | tf_op jit(solution)/shard_map/ppermute | solution.py:37
  208.9 0.9 fusion.4
  (2 shorter events, 0.1 us)
Async XLA Ops:
  0.6 9.6 %copy-start.2 = (s32[16,2]{0,1:T(2,128)S(1)}, s32[16,2]{0,1:T(2,128)}, u32[]{:S(2)}) copy-start(s32[16,2]{0,1:T(2,128)} %param.8) | copy-start | bytes 388
  3.8 29.7 %collective-permute-start = (f32[2,256,1024]{2,1,0:T(8,128)}, f32[2,256,1024]{2,1,0:T(8,128)S(1)}, u32[]{:S(2)}, u32[]{:S(2)}) collective-permute-start(f32[2,256,1024]{2,1,0:T(8,128)} %slice.35), channel_id=1, source_target_pairs={{1,0},{2,1},{3,2},{4,3},{5,4},{6,5},{7,6},{8,7},{9,8},{10,9},{11,1... | collective-permute-start | bytes 6291464 | tf_op jit(solution)/shard_map/ppermute | solution.py:17
  33.5 1.4 copy-start
  73.5 32.0 %collective-permute-start.1 = (f32[8,2,256,128]{3,2,1,0:T(8,128)S(1)}, f32[8,2,256,128]{3,2,1,0:T(8,128)S(1)}, u32[]{:S(2)}, u32[]{:S(2)}) collective-permute-start(f32[8,2,256,128]{3,2,1,0:T(8,128)S(1)} %slice.37), channel_id=1, source_target_pairs={{0,1},{1,2},{2,3},{3,4},{4,5},{5,6},{6,7},{7,8},{8,9},{9,10},{10,1... | collective-permute-start | bytes 6291464 | tf_op jit(solution)/shard_map/ppermute | solution.py:17
  108.5 1.5 copy-start.1
  108.6 45.1 %collective-permute-start.2 = (f32[2,2,2,512,128]{4,3,2,0,1:T(8,128)S(1)}, f32[2,2,2,512,128]{4,3,2,0,1:T(8,128)S(1)}, u32[]{:S(2)}, u32[]{:S(2)}) collective-permute-start(f32[2,2,2,512,128]{4,3,2,0,1:T(8,128)S(1)} %bitcast.52), channel_id=1, source_target_pairs={{0,32},{32,0},{64,96},{96,64},{128,160},{160,128},{192,224},{224,1... | collective-permute-start | bytes 6291464 | tf_op jit(solution)/shard_map/ppermute | solution.py:37
  109.9 11.9 %collective-permute-start.5 = (f32[2,256,256]{2,1,0:T(8,128)S(1)}, f32[2,256,256]{2,1,0:T(8,128)S(1)}, u32[]{:S(2)}, u32[]{:S(2)}) collective-permute-start(f32[2,256,256]{2,1,0:T(8,128)S(1)} %copy-done.1), channel_id=1, source_target_pairs={{0,8},{1,9},{2,10},{3,11},{4,12},{5,13},{6,14},{7,15},{8,0},{9,1},... | collective-permute-start | bytes 1572872 | tf_op jit(solution)/shard_map/ppermute | solution.py:26
  121.9 25.2 %collective-permute-start.6 = (f32[2,256,256]{2,1,0:T(8,128)S(1)}, f32[2,256,256]{2,1,0:T(8,128)S(1)}, u32[]{:S(2)}, u32[]{:S(2)}) collective-permute-start(f32[2,256,256]{2,1,0:T(8,128)S(1)} %add.78), channel_id=1, source_target_pairs={{0,16},{1,17},{2,18},{3,19},{4,20},{5,21},{6,22},{7,23},{8,24},{9,... | collective-permute-start | bytes 1572872 | tf_op jit(solution)/shard_map/ppermute | solution.py:26
  147.2 9.7 %collective-permute-start.7 = (f32[2,256,256]{2,1,0:T(8,128)S(1)}, f32[2,256,256]{2,1,0:T(8,128)S(1)}, u32[]{:S(2)}, u32[]{:S(2)}) collective-permute-start(f32[2,256,256]{2,1,0:T(8,128)S(1)} %add.79), channel_id=1, source_target_pairs={{0,1},{1,0},{2,3},{3,2},{4,5},{5,4},{6,7},{7,6},{8,9},{9,8},{10,11... | collective-permute-start | bytes 1572872 | tf_op jit(solution)/shard_map/ppermute | solution.py:26
  154.1 25.6 %collective-permute-start.3 = (f32[2,2,512,128]{3,2,1,0:T(8,128)S(1)}, f32[2,2,512,128]{3,2,1,0:T(8,128)S(1)}, u32[]{:S(2)}, u32[]{:S(2)}) collective-permute-start(f32[2,2,512,128]{3,2,1,0:T(8,128)S(1)} %slice_bitcast_fusion), channel_id=1, source_target_pairs={{0,64},{32,96},{64,0},{96,32},{128,192},{160,224},{192,128},{224,1... | collective-permute-start | bytes 3145736 | tf_op jit(solution)/shard_map/ppermute | solution.py:37
  157.0 13.1 %collective-permute-start.8 = (f32[2,256,256]{2,1,0:T(8,128)S(1)}, f32[2,256,256]{2,1,0:T(8,128)S(1)}, u32[]{:S(2)}, u32[]{:S(2)}) collective-permute-start(f32[2,256,256]{2,1,0:T(8,128)S(1)} %add.80), channel_id=1, source_target_pairs={{0,2},{1,3},{2,0},{3,1},{4,6},{5,7},{6,4},{7,5},{8,10},{9,11},{10,... | collective-permute-start | bytes 1572872 | tf_op jit(solution)/shard_map/ppermute | solution.py:26
  170.2 16.6 %collective-permute-start.9 = (f32[2,256,256]{2,1,0:T(8,128)S(1)}, f32[2,256,256]{2,1,0:T(8,128)S(1)}, u32[]{:S(2)}, u32[]{:S(2)}) collective-permute-start(f32[2,256,256]{2,1,0:T(8,128)S(1)} %add.81), channel_id=1, source_target_pairs={{0,4},{1,5},{2,6},{3,7},{4,0},{5,1},{6,2},{7,3},{8,12},{9,13},{10,... | collective-permute-start | bytes 1572872 | tf_op jit(solution)/shard_map/ppermute | solution.py:26
  179.8 29.1 %collective-permute-start.4 = (f32[2,512,128]{2,1,0:T(8,128)S(1)}, f32[2,512,128]{2,1,0:T(8,128)S(1)}, u32[]{:S(2)}, u32[]{:S(2)}) collective-permute-start(f32[2,512,128]{2,1,0:T(8,128)S(1)} %slice_bitcast_fusion.2), channel_id=1, source_target_pairs={{0,128},{32,160},{64,192},{96,224},{128,0},{160,32},{192,64},{224,... | collective-permute-start | bytes 1572872 | tf_op jit(solution)/shard_map/ppermute | solution.py:37

commit v3 on v2

--- a/solution.py
+++ b/solution.py
@@ -27,14 +27,27 @@
     return block
 
 
-def sum_scatter_blocks(held, axis):
-    bits = lax.axis_size(axis).bit_length() - 1
+def sum_scatter_blocks(held, axis, other):
+    count = lax.axis_size(axis)
+    others = lax.axis_size(other)
+    bits = count.bit_length() - 1
+    odd = lax.axis_index(other) % 2 == 1
     held = held.reshape((2,) * bits + held.shape[1:])
     for bit in range(bits):
         place = bits - 1 - bit
         kept = lax.index_in_dim(held, 0, place, keepdims=False)
         sent = lax.index_in_dim(held, 1, place, keepdims=False)
-        held = kept + lax.ppermute(sent, axis, xor_route(axis, bit))
+        if bit == 0 and bits >= 2:
+            route = [
+                (w * others + r, (w ^ (1 if r % 2 == 0 else 3)) * others + r)
+                for w in range(count)
+                for r in range(others)
+            ]
+            got = lax.ppermute(sent, (axis, other), route)
+            got = jnp.where(odd, jnp.flip(got, axis=place - 1), got)
+        else:
+            got = lax.ppermute(sent, axis, xor_route(axis, bit))
+        held = kept + got
     return held
 
 
@@ -284,7 +297,7 @@
     tile_grad = grad_ext[:, :, :tile_rows, :] + jnp.pad(
         arrived, ((0, 0), (0, 0), (0, tile_rows - patch_side), (0, 0))
     )
-    object_out = sum_scatter_blocks(tile_grad, "wave")
+    object_out = sum_scatter_blocks(tile_grad, "wave", "region")
     return (object_out, probe_total[None])
 
 

time: 210 us -> 210 us (level)
  the two profiles are of different devices: /device:TPU:25 before, /device:TPU:8 now
where the time goes in v3:
time: 210 us; the launch traced here: 208 us
  waiting for transfers between devices  128 us (61%)
  Pallas kernels  40.4 us (19%)
  starting transfers between devices  18.1 us (9%)
  other arithmetic  11.8 us (6%)
  local copies, waits for them, and re-layouts  8.17 us (4%)
    ppermute x2, waiting for transfers between devices, from_behind(): return lax.ppermute(block, axis, route)  47.8 us
    ppermute x5, waiting for transfers between devices, sum_over(): block = block + lax.ppermute(block, axis, xor_route(axis, bit))  44.2 us
    pallas_call x1, Pallas kernels, fused_step(): pl.pallas_call(fused_kernel, grid_spec=grid_spec, out_shape=(jax.ShapeDty...  40.4 us
    ppermute x2, waiting for transfers between devices, sum_scatter_blocks(): got = lax.ppermute(sent, axis, xor_route(axis, bit))  36.1 us
    ppermute x5, starting transfers between devices, sum_over(): block = block + lax.ppermute(block, axis, xor_route(axis, bit))  8.6 us
    ppermute x2, starting transfers between devices, sum_scatter_blocks(): got = lax.ppermute(sent, axis, xor_route(axis, bit))  4.23 us
  transfers between devices with their start and end apart: 10, of which 7 were waited for; matrix products, arithmetic and copies ran while one was open for 4% of the time, Pallas kernels for 0%

profile of v3, /device:TPU:8, one launch (start us, length us, event | category | flops | bytes accessed | tf_op | source)
XLA Modules:
  0.0 208.1 jit_solution(1926446224217422481)
XLA Ops:
  0.6 0.0 copy-start.2
  0.6 3.2 %slice.35 = f32[2,256,1024]{2,1,0:T(8,128)} slice(f32[2,512,1024]{2,1,0:T(8,128)} %tile_ref.1), slice={[0:2], [0:256], [0:1024]} | slice | bytes 4194304 | tf_op jit(solution)/shard_map/slice | solution.py:280
  3.8 1.9 collective-permute-start
  6.4 1.0 fusion.11
  7.4 1.1 multiply_convert_fusion
  8.5 1.0 fusion.3
  9.6 0.0 copy-done.2
  9.6 0.6 bitcast_subtract_fusion
  10.2 0.7 add_xor_fusion.place_ref
  10.9 18.7 %collective-permute-done.rim_ref = f32[2,256,1024]{2,1,0:T(8,128)S(1)} collective-permute-done((f32[2,256,1024]{2,1,0:T(8,128)}, f32[2,256,1024]{2,1,0:T(8,128)S(1)}, u32[]{:S(2)}, u32[]{:S(2)}) %collective-permute-start) | collective-permute-done | bytes 2097184 | tf_op jit(solution)/shard_map/ppermute | solution.py:17
  29.6 0.0 copy-start
  29.6 1.3 copy-done
  30.9 40.4 %shard_map.68 = (f32[8,2,768,128]{3,2,1,0:T(8,128)}, f32[2,256,256]{2,1,0:T(8,128)}) custom-call(s32[16]{0:T(128)} %get-tuple-element.15.base_ref, s32[16]{0:T(128)} %get-tuple-element.14.down_ref, s32[16]{0:T(128)} %get-tuple-element.7.start_ref, s32[16]{0:T(128)} %get-tuple-element.6.shift_ref, s32[16,3]{1,0:T(8,128)} %add_xor_fusion.place_ref, ...), custom_call_target="tpu_custom_call" | custom-call | tf_op jit(solution)/shard_map/pallas_call | solution.py:235
  71.4 1.7 slice.37
  73.1 1.9 collective-permute-start.1
  75.1 29.1 %collective-permute-done.1 = f32[8,2,256,128]{3,2,1,0:T(8,128)S(1)} collective-permute-done((f32[8,2,256,128]{3,2,1,0:T(8,128)S(1)}, f32[8,2,256,128]{3,2,1,0:T(8,128)S(1)}, u32[]{:S(2)}, u32[]{:S(2)}) %collective-permute-start.1) | collective-permute-done | bytes 2097184 | tf_op jit(solution)/shard_map/ppermute | solution.py:17
  104.1 2.7 %pad_add_fusion = f32[8,2,512,128]{3,2,1,0:T(8,128)S(1)} fusion(f32[8,2,256,128]{3,2,1,0:T(8,128)S(1)} %collective-permute-done.1, f32[8,2,768,128]{3,2,1,0:T(8,128)} %get-tuple-element.4), kind=kLoop, calls=%fused_computation | loop fusion | flops 1048576 | bytes 10485760 | tf_op jit(solution)/shard_map/add | solution.py:297
  106.8 0.3 fusion.15
  107.1 0.0 copy-start.1
  107.1 1.5 copy.15
  108.6 1.5 collective-permute-start.2
  110.1 0.0 copy-done.1
  110.1 2.0 collective-permute-start.5
  112.1 7.2 %collective-permute-done.5 = f32[2,256,256]{2,1,0:T(8,128)S(1)} collective-permute-done((f32[2,256,256]{2,1,0:T(8,128)S(1)}, f32[2,256,256]{2,1,0:T(8,128)S(1)}, u32[]{:S(2)}, u32[]{:S(2)}) %collective-permute-start.5) | collective-permute-done | bytes 524320 | tf_op jit(solution)/shard_map/ppermute | solution.py:26
  119.3 0.1 add.83
  119.4 6.1 %collective-permute-start.6 = (f32[2,256,256]{2,1,0:T(8,128)S(1)}, f32[2,256,256]{2,1,0:T(8,128)S(1)}, u32[]{:S(2)}, u32[]{:S(2)}) collective-permute-start(f32[2,256,256]{2,1,0:T(8,128)S(1)} %add.83), channel_id=1, source_target_pairs={{0,16},{1,17},{2,18},{3,19},{4,20},{5,21},{6,22},{7,23},{8,24},{9,... | collective-permute-start | bytes 1572872 | tf_op jit(solution)/shard_map/ppermute | solution.py:26
  125.5 22.9 %collective-permute-done.6 = f32[2,256,256]{2,1,0:T(8,128)S(1)} collective-permute-done((f32[2,256,256]{2,1,0:T(8,128)S(1)}, f32[2,256,256]{2,1,0:T(8,128)S(1)}, u32[]{:S(2)}, u32[]{:S(2)}) %collective-permute-start.6) | collective-permute-done | bytes 524320 | tf_op jit(solution)/shard_map/ppermute | solution.py:26
  148.5 0.1 add.84
  148.5 0.1 collective-permute-start.7
  148.6 0.0 collective-permute-done.2
  148.6 2.5 %fusion = f32[2,2,2,512,128]{4,3,2,0,1:T(8,128)S(1)} fusion(f32[2,2,2,512,128]{4,3,2,0,1:T(8,128)} %collective-permute-done.2, f32[2,2,1,2,512,128]{5,4,3,2,1,0:T(8,128)S(1)} %get-tuple-element.10, pred[]{:T(512)S(6)} %eq.7), kind=kLoop, calls=%fused_computation.2 | loop fusion | flops 1048576 | bytes 6291457 | tf_op jit(solution)/shard_map/add | solution.py:50
  151.2 0.1 slice_bitcast_fusion
  151.2 0.1 collective-permute-start.3
  151.3 0.0 collective-permute-done.7
  151.3 0.1 add.85
  151.4 0.3 collective-permute-start.8
  151.7 14.1 %collective-permute-done.8 = f32[2,256,256]{2,1,0:T(8,128)S(1)} collective-permute-done((f32[2,256,256]{2,1,0:T(8,128)S(1)}, f32[2,256,256]{2,1,0:T(8,128)S(1)}, u32[]{:S(2)}, u32[]{:S(2)}) %collective-permute-start.8) | collective-permute-done | bytes 524320 | tf_op jit(solution)/shard_map/ppermute | solution.py:26
  165.8 0.1 add.86
  165.9 0.1 collective-permute-start.9
  166.0 12.4 %collective-permute-done.3 = f32[2,2,512,128]{3,2,1,0:T(8,128)S(1)} collective-permute-done((f32[2,2,512,128]{3,2,1,0:T(8,128)S(1)}, f32[2,2,512,128]{3,2,1,0:T(8,128)S(1)}, u32[]{:S(2)}, u32[]{:S(2)}) %collective-permute-start.3) | collective-permute-done | bytes 1048608 | tf_op jit(solution)/shard_map/ppermute | solution.py:49
  178.4 0.1 fusion.1
  178.6 4.1 %collective-permute-start.4 = (f32[2,512,128]{2,1,0:T(8,128)S(1)}, f32[2,512,128]{2,1,0:T(8,128)S(1)}, u32[]{:S(2)}, u32[]{:S(2)}) collective-permute-start(f32[2,512,128]{2,1,0:T(8,128)S(1)} %slice_bitcast_fusion.2), channel_id=1, source_target_pairs={{0,128},{32,160},{64,192},{96,224},{128,0},{160,32},{192,64},{224,... | collective-permute-start | bytes 1572872 | tf_op jit(solution)/shard_map/ppermute | solution.py:49
  182.7 0.0 collective-permute-done.9
  182.7 0.9 add_bitcast_fusion
  183.6 23.7 %collective-permute-done.4 = f32[2,512,128]{2,1,0:T(8,128)S(1)} collective-permute-done((f32[2,512,128]{2,1,0:T(8,128)S(1)}, f32[2,512,128]{2,1,0:T(8,128)S(1)}, u32[]{:S(2)}, u32[]{:S(2)}) %collective-permute-start.4) | collective-permute-done | bytes 524320 | tf_op jit(solution)/shard_map/ppermute | solution.py:49
  207.3 0.8 fusion.4
  (2 shorter events, 0.1 us)
Async XLA Ops:
  0.6 8.9 %copy-start.2 = (s32[16,2]{0,1:T(2,128)S(1)}, s32[16,2]{0,1:T(2,128)}, u32[]{:S(2)}) copy-start(s32[16,2]{0,1:T(2,128)} %param.8) | copy-start | bytes 388
  3.8 25.8 %collective-permute-start = (f32[2,256,1024]{2,1,0:T(8,128)}, f32[2,256,1024]{2,1,0:T(8,128)S(1)}, u32[]{:S(2)}, u32[]{:S(2)}) collective-permute-start(f32[2,256,1024]{2,1,0:T(8,128)} %slice.35), channel_id=1, source_target_pairs={{1,0},{2,1},{3,2},{4,3},{5,4},{6,5},{7,6},{8,7},{9,8},{10,9},{11,1... | collective-permute-start | bytes 6291464 | tf_op jit(solution)/shard_map/ppermute | solution.py:17
  29.6 1.4 copy-start
  73.1 31.0 %collective-permute-start.1 = (f32[8,2,256,128]{3,2,1,0:T(8,128)S(1)}, f32[8,2,256,128]{3,2,1,0:T(8,128)S(1)}, u32[]{:S(2)}, u32[]{:S(2)}) collective-permute-start(f32[8,2,256,128]{3,2,1,0:T(8,128)S(1)} %slice.37), channel_id=1, source_target_pairs={{0,1},{1,2},{2,3},{3,4},{4,5},{5,6},{6,7},{7,8},{8,9},{9,10},{10,1... | collective-permute-start | bytes 6291464 | tf_op jit(solution)/shard_map/ppermute | solution.py:17
  107.1 3.0 %copy-start.1 = (f32[2,256,256]{2,1,0:T(8,128)S(1)}, f32[2,256,256]{2,1,0:T(8,128)}, u32[]{:S(2)}) copy-start(f32[2,256,256]{2,1,0:T(8,128)} %get-tuple-element.5) | copy-start | bytes 1572868
  108.6 40.0 %collective-permute-start.2 = (f32[2,2,2,512,128]{4,3,2,0,1:T(8,128)}, f32[2,2,2,512,128]{4,3,2,0,1:T(8,128)}, u32[]{:S(2)}, u32[]{:S(2)}) collective-permute-start(f32[2,2,2,512,128]{4,3,2,0,1:T(8,128)} %bitcast.49), channel_id=1, source_target_pairs={{0,32},{1,97},{2,34},{3,99},{4,36},{5,101},{6,38},{7,103},{8,40},{... | collective-permute-start | bytes 6291464 | tf_op jit(solution)/shard_map/ppermute | solution.py:46
  110.1 9.2 %collective-permute-start.5 = (f32[2,256,256]{2,1,0:T(8,128)S(1)}, f32[2,256,256]{2,1,0:T(8,128)S(1)}, u32[]{:S(2)}, u32[]{:S(2)}) collective-permute-start(f32[2,256,256]{2,1,0:T(8,128)S(1)} %copy-done.1), channel_id=1, source_target_pairs={{0,8},{1,9},{2,10},{3,11},{4,12},{5,13},{6,14},{7,15},{8,0},{9,1},... | collective-permute-start | bytes 1572872 | tf_op jit(solution)/shard_map/ppermute | solution.py:26
  119.4 29.1 %collective-permute-start.6 = (f32[2,256,256]{2,1,0:T(8,128)S(1)}, f32[2,256,256]{2,1,0:T(8,128)S(1)}, u32[]{:S(2)}, u32[]{:S(2)}) collective-permute-start(f32[2,256,256]{2,1,0:T(8,128)S(1)} %add.83), channel_id=1, source_target_pairs={{0,16},{1,17},{2,18},{3,19},{4,20},{5,21},{6,22},{7,23},{8,24},{9,... | collective-permute-start | bytes 1572872 | tf_op jit(solution)/shard_map/ppermute | solution.py:26
  148.5 2.8 %collective-permute-start.7 = (f32[2,256,256]{2,1,0:T(8,128)S(1)}, f32[2,256,256]{2,1,0:T(8,128)S(1)}, u32[]{:S(2)}, u32[]{:S(2)}) collective-permute-start(f32[2,256,256]{2,1,0:T(8,128)S(1)} %add.84), channel_id=1, source_target_pairs={{0,1},{1,0},{2,3},{3,2},{4,5},{5,4},{6,7},{7,6},{8,9},{9,8},{10,11... | collective-permute-start | bytes 1572872 | tf_op jit(solution)/shard_map/ppermute | solution.py:26
  151.2 27.1 %collective-permute-start.3 = (f32[2,2,512,128]{3,2,1,0:T(8,128)S(1)}, f32[2,2,512,128]{3,2,1,0:T(8,128)S(1)}, u32[]{:S(2)}, u32[]{:S(2)}) collective-permute-start(f32[2,2,512,128]{3,2,1,0:T(8,128)S(1)} %slice_bitcast_fusion), channel_id=1, source_target_pairs={{0,64},{32,96},{64,0},{96,32},{128,192},{160,224},{192,128},{224,1... | collective-permute-start | bytes 3145736 | tf_op jit(solution)/shard_map/ppermute | solution.py:49
  151.4 14.4 %collective-permute-start.8 = (f32[2,256,256]{2,1,0:T(8,128)S(1)}, f32[2,256,256]{2,1,0:T(8,128)S(1)}, u32[]{:S(2)}, u32[]{:S(2)}) collective-permute-start(f32[2,256,256]{2,1,0:T(8,128)S(1)} %add.85), channel_id=1, source_target_pairs={{0,2},{1,3},{2,0},{3,1},{4,6},{5,7},{6,4},{7,5},{8,10},{9,11},{10,... | collective-permute-start | bytes 1572872 | tf_op jit(solution)/shard_map/ppermute | solution.py:26
  165.9 16.8 %collective-permute-start.9 = (f32[2,256,256]{2,1,0:T(8,128)S(1)}, f32[2,256,256]{2,1,0:T(8,128)S(1)}, u32[]{:S(2)}, u32[]{:S(2)}) collective-permute-start(f32[2,256,256]{2,1,0:T(8,128)S(1)} %add.86), channel_id=1, source_target_pairs={{0,4},{1,5},{2,6},{3,7},{4,0},{5,1},{6,2},{7,3},{8,12},{9,13},{10,... | collective-permute-start | bytes 1572872 | tf_op jit(solution)/shard_map/ppermute | solution.py:26
  178.6 28.7 %collective-permute-start.4 = (f32[2,512,128]{2,1,0:T(8,128)S(1)}, f32[2,512,128]{2,1,0:T(8,128)S(1)}, u32[]{:S(2)}, u32[]{:S(2)}) collective-permute-start(f32[2,512,128]{2,1,0:T(8,128)S(1)} %slice_bitcast_fusion.2), channel_id=1, source_target_pairs={{0,128},{32,160},{64,192},{96,224},{128,0},{160,32},{192,64},{224,... | collective-permute-start | bytes 1572872 | tf_op jit(solution)/shard_map/ppermute | solution.py:49
